TPU v7x, 128 devices: a whole 4x4x4 slice. The times are simulated.
128 devices in a mesh: dp: 4 (over y_hi, core), mp: 32 (over x, z, y_lo).
Axes of the slice: x: 4, y: 4 (y_hi: 2, y_lo: 2; y = y_hi * 2 + y_lo), z: 4, core: 2. Of those that a mesh axis runs over, the one named last changes fastest.
Arguments:
- tokens: bfloat16 [8192, 3072], P(('dp', 'mp')), may hold values from -6 to 6
- cotangent: bfloat16 [8192, 3072], P(('dp', 'mp')), may hold values from -3 to 3
- w_qkv: bfloat16 [3072, 32, 384], P(None, 'mp'), may hold values from -0.109375 to 0.109375
- w_out: bfloat16 [32, 128, 3072], P('mp'), may hold values from -0.09375 to 0.09375
- moment_qkv: float32 [3072, 32, 384], P('dp', 'mp'), may hold values from -6 to 6
- second_qkv: float32 [3072, 32, 384], P('dp', 'mp'), may hold values from 0.01 to 100
- moment_out: float32 [32, 128, 3072], P('mp', None, 'dp'), may hold values from -6 to 6
- second_out: float32 [32, 128, 3072], P('mp', None, 'dp'), may hold values from 0.01 to 100
Outputs:
- input_grad: bfloat16 [8192, 3072], P(('dp', 'mp'))
- new_moment_qkv: float32 [3072, 32, 384], P('dp', 'mp')
- new_second_qkv: float32 [3072, 32, 384], P('dp', 'mp')
- update_qkv: float32 [3072, 32, 384], P('dp', 'mp')
- new_moment_out: float32 [32, 128, 3072], P('mp', None, 'dp')
- new_second_out: float32 [32, 128, 3072], P('mp', None, 'dp')
- update_out: float32 [32, 128, 3072], P('mp', None, 'dp')
All inputs are finite; a program needn't handle non-finite values.
Results may differ from a plain program's by a relative error of at most 0.035.
Values may be sent and summed in bfloat16 or wider, within the bound.
No kernel may reach another device: no remote copies, remote signals or barrier semaphores. Data moves between devices by JAX's collectives and lax.ppermute only.
A program may use at most 128 MiB of HBM per device.

v0:
```python
from functools import partial
import math
import jax
import jax.numpy as jnp
from jax import lax
from jax.sharding import PartitionSpec as P

SEQ = 256
beta_one = 0.9
beta_two = 0.95
step_count = 10
eps_base = 0.001
norm_eps = 1e-06


def normalize(block):
    centre = block - jnp.mean(block, axis=-1, keepdims=True)
    return centre / jnp.sqrt(jnp.mean(centre * centre, axis=-1, keepdims=True) + norm_eps)


def attend(packed, seq):
    head_width = packed.shape[1] // 3
    blocks = packed.reshape(packed.shape[0] // seq, seq, 3 * head_width)
    query_rows = normalize(blocks[:, :, :head_width])
    key_matrix_rows = normalize(blocks[:, :, head_width : 2 * head_width])
    value_matrix_rows = blocks[:, :, 2 * head_width :]
    attention_scores = jnp.einsum("oaw,ozw->oaz", query_rows, key_matrix_rows) / math.sqrt(
        head_width
    )
    attention_weights = jnp.exp(attention_scores)
    attention_weights = attention_weights / jnp.sum(attention_weights, axis=-1, keepdims=True)
    mixed_heads_output = jnp.einsum("ryn,rni->ryi", attention_weights, value_matrix_rows)
    return mixed_heads_output.reshape(packed.shape[0], head_width)


def adam_step(grad, moment, second, fan_in):
    new_moment = beta_one * moment + (1.0 - beta_one) * grad
    new_second = beta_two * second + (1.0 - beta_two) * grad * grad
    corrected = new_moment / (1.0 - beta_one**step_count)
    scaled = new_second / (1.0 - beta_two**step_count)
    update = -corrected / (jnp.sqrt(scaled) + eps_base / math.sqrt(fan_in))
    return (new_moment, new_second, update)


def shards(tokens, cotangent, w_qkv, w_out, moment_qkv, second_qkv, moment_out, second_out):
    rows = lax.all_gather(tokens, "mp", axis=0, tiled=True)
    cot_rows = lax.all_gather(cotangent, "mp", axis=0, tiled=True)
    projection = w_qkv[:, 0, :]
    out_rows = w_out[0]
    packed = jnp.dot(rows, projection, preferred_element_type=jnp.float32).astype(jnp.bfloat16)
    mixed_heads_output, backward = jax.vjp(partial(attend, seq=SEQ), packed.astype(jnp.float32))
    mixed_low = mixed_heads_output.astype(jnp.bfloat16)
    dmix = jnp.dot(cot_rows, out_rows.T, preferred_element_type=jnp.float32).astype(jnp.bfloat16)
    out_part = jnp.dot(mixed_low.T, cot_rows, preferred_element_type=jnp.float32)
    packed_grad = backward(dmix.astype(jnp.float32))[0].astype(jnp.bfloat16)
    qkv_part = jnp.dot(rows.T, packed_grad, preferred_element_type=jnp.float32)
    whole_term = jnp.dot(packed_grad, projection.T, preferred_element_type=jnp.float32)
    input_grad = lax.psum_scatter(
        whole_term.astype(jnp.bfloat16), "mp", scatter_dimension=0, tiled=True
    )
    summed_qkv, summed_out = (
        lax.psum_scatter(
            qkv_part[:, None, :].astype(jnp.bfloat16), "dp", scatter_dimension=0, tiled=True
        ).astype(jnp.float32),
        lax.psum_scatter(
            out_part[None].astype(jnp.bfloat16), "dp", scatter_dimension=2, tiled=True
        ).astype(jnp.float32),
    )
    width_in = w_qkv.shape[0]
    heads_width = w_out.shape[0] * w_out.shape[1] * lax.axis_size("mp")
    m_qkv, s_qkv, u_qkv = adam_step(summed_qkv, moment_qkv, second_qkv, width_in)
    m_out, s_out, u_out = adam_step(summed_out, moment_out, second_out, heads_width)
    return (input_grad, m_qkv, s_qkv, u_qkv, m_out, s_out, u_out)


def solution(mesh):
    placed = (
        P(("dp", "mp"), None),
        P(("dp", "mp"), None),
        P(None, "mp", None),
        P("mp", None, None),
        P("dp", "mp", None),
        P("dp", "mp", None),
        P("mp", None, "dp"),
        P("mp", None, "dp"),
    )
    return jax.shard_map(
        shards,
        mesh=mesh,
        in_specs=placed,
        out_specs=(
            P(("dp", "mp"), None),
            P("dp", "mp", None),
            P("dp", "mp", None),
            P("dp", "mp", None),
            P("mp", None, "dp"),
            P("mp", None, "dp"),
            P("mp", None, "dp"),
        ),
        check_vma=False,
    )
```

profile of v0, /device:TPU:0, one launch (start us, length us, event | category | flops | bytes accessed | tf_op | source)
XLA Modules:
  0.0 927.5 jit_solution(5022044100297365708)
XLA Ops:
  8.7 277.4 %all-gather.3.cloned.1.call-done = bf16[2048,3072]{1,0:T(8,128)(2,1)} async-done(((bf16[64,3072]{1,0:T(8,128)(2,1)}), bf16[2048,3072]{1,0:T(8,128)(2,1)}) %all-gather.3.cloned.1.call-update) | async-done | bytes 12582928 | tf_op jit(solution)/shard_map/all_gather | solution.py:46
  286.1 9.6 %bitcast_convert_fusion = (f32[8,256,384]{2,1,0:T(8,128)S(1)}, bf16[2048,384]{1,0:T(8,128)(2,1)S(1)}) fusion(bf16[2048,3072]{1,0:T(8,128)(2,1)} %all-gather.3.cloned.1.call-done, bf16[3072,1,384]{2,0,1:T(8,128)(2,1)S(1)} %copy-done), kind=kOutput, calls=%fused_computation.59 | convolution fusion | flops 4833411072 | bytes 19660800 | tf_op jit(solution)/shard_map/dot_general | solution.py:50
  296.3 1.3 multiply_reduce_fusion.4
  297.7 2.8 fusion.29
  300.6 1.4 copy-done.4
  302.5 260.6 %all-gather.5.cloned.1.call-done = bf16[2048,3072]{1,0:T(8,128)(2,1)} async-done(((bf16[64,3072]{1,0:T(8,128)(2,1)}), bf16[2048,3072]{1,0:T(8,128)(2,1)}) %all-gather.5.cloned.1.call-update) | async-done | bytes 12582928 | tf_op jit(solution)/shard_map/all_gather | solution.py:47
  563.0 7.3 fusion.1
  570.6 8.3 convolution_convert_fusion.4
  578.9 1.7 multiply_reduce_fusion
  581.1 3.1 multiply_reduce_fusion.2
  584.2 4.0 fusion.23
  588.2 1.3 fusion.24
  589.5 2.6 broadcast_add_fusion.1
  593.9 6.4 fusion
  600.6 11.2 %convolution_convert_fusion = bf16[2048,3072]{1,0:T(8,128)(2,1)} fusion(bf16[2048,384]{1,0:T(8,128)(2,1)} %bitcast.31, bf16[3072,1,384]{2,0,1:T(8,128)(2,1)S(1)} %copy-done), kind=kOutput, calls=%fused_computation | convolution fusion | flops 4838129664 | bytes 16515072 | tf_op jit(solution)/shard_map/dot_general | solution.py:57
  611.8 3.4 copy.16
  615.3 4.7 copy.17
  620.0 2.4 add_divide_fusion.1
  622.3 21.8 %reduce-scatter.6.cloned.1.call-done = bf16[768,1,384]{0,2,1:T(8,128)(2,1)} async-done(((bf16[3072,1,384]{0,2,1:T(8,128)(2,1)}), bf16[768,1,384]{0,2,1:T(8,128)(2,1)}) %reduce-scatter.6.cloned.1.call-update) | async-done | bytes 589840 | tf_op jit(solution)/shard_map/reduce_scatter | solution.py:62
  644.2 3.7 add_divide_fusion
  647.8 4.8 copy.21
  652.6 4.7 copy.20
  657.3 2.6 copy.19
  660.0 261.0 %reduce-scatter.4.cloned.1.call-done = bf16[64,3072]{1,0:T(8,128)(2,1)} async-done(((bf16[2048,3072]{1,0:T(8,128)(2,1)}), bf16[64,3072]{1,0:T(8,128)(2,1)}) %reduce-scatter.4.cloned.1.call-update) | async-done | bytes 393232 | tf_op jit(solution)/shard_map/reduce_scatter | solution.py:58
  (46 shorter events, 5.5 us)
Async XLA Ops:
  7.2 278.9 %copy-start = (bf16[3072,1,384]{2,0,1:T(8,128)(2,1)S(1)}, bf16[3072,1,384]{2,0,1:T(8,128)(2,1)}, u32[]{:S(2)}) copy-start(bf16[3072,1,384]{2,0,1:T(8,128)(2,1)} %param.10) | copy-start | bytes 7077892
  7.2 278.9 %all-gather.3.cloned.1.call-start = ((), (), s32[]{:S(2)}) async-start(), calls=%async_computation.3 | async-start | bytes 12976128 | tf_op jit(solution)/shard_map/all_gather | solution.py:46
  7.9 555.1 %all-gather.5.cloned.1.call-start = ((), (), s32[]{:S(2)}) async-start(), calls=%async_computation.4 | async-start | bytes 12976128 | tf_op jit(solution)/shard_map/all_gather | solution.py:47
  8.7 611.3 %reduce-scatter.8.cloned.1.call-start = ((), (), s32[]{:S(2)}) async-start(), calls=%async_computation.7 | async-start | bytes 983040 | tf_op jit(solution)/shard_map/reduce_scatter | solution.py:65
  295.7 2.0 copy-start.1
  295.7 4.8 copy-start.7
  300.5 1.4 copy-start.4
  570.3 73.8 %reduce-scatter.6.cloned.1.call-start = ((), (), s32[]{:S(2)}) async-start(), calls=%async_computation.6 | async-start | bytes 2949120 | tf_op jit(solution)/shard_map/reduce_scatter | solution.py:62
  570.6 8.3 copy-start.5
  578.9 2.2 copy-start.2
  584.2 9.7 %slice-start = ((s8[12582912]{0:T(1024)(128)(4,1)}), s8[4194304]{0:T(1024)(128)(4,1)S(1)}, s32[]{:S(2)}) async-start(s8[12582912]{0:T(1024)(128)(4,1)} %bitcast.37), calls=%async_computation.8 | async-start | bytes 8388608
  584.2 9.7 %slice-start.1 = ((s8[12582912]{0:T(1024)(128)(4,1)}), s8[4194304]{0:T(1024)(128)(4,1)S(1)}, s32[]{:S(2)}) async-start(s8[12582912]{0:T(1024)(128)(4,1)} %bitcast.37), calls=%async_computation.9 | async-start | bytes 8388608
  589.5 4.4 slice-start.2
  592.7 1.2 copy-start.6
  600.4 320.6 %reduce-scatter.4.cloned.1.call-start = ((), (), s32[]{:S(2)}) async-start(), calls=%async_computation.5 | async-start | bytes 12976128 | tf_op jit(solution)/shard_map/reduce_scatter | solution.py:58
  647.8 9.5 %copy-start.3 = (f32[768,1,384]{0,2,1:T(8,128)S(1)}, f32[768,1,384]{0,2,1:T(8,128)}, u32[]{:S(2)}) copy-start(f32[768,1,384]{0,2,1:T(8,128)} %get-tuple-element.25) | copy-start | bytes 3538948
Sparse Core Ops, SparseCore 0:
  9.7 276.3 all-gather.2
  287.7 275.2 all-gather.4
  570.4 31.5 reduce-scatter.7
  604.8 39.3 reduce-scatter.5
  647.0 273.9 reduce-scatter.3
where the time goes:
time: 928 us
  waiting for transfers between devices  822 us (89%)
  matrix products  55.3 us (6%)
  local copies, waits for them, and re-layouts  23.3 us (3%)
  between operations  14.1 us (2%)
  other arithmetic  12 us (1%)
    all_gather x1, waiting for transfers between devices, shards(): rows = lax.all_gather(tokens, 'mp', axis=0, tiled=True)  277 us
    reduce_scatter x1, waiting for transfers between devices, shards(): lax.psum_scatter(whole_term.astype(jnp.bfloat16), 'mp', scatter_dimension...  261 us
    all_gather x1, waiting for transfers between devices, shards(): cot_rows = lax.all_gather(cotangent, 'mp', axis=0, tiled=True)  261 us
    unnamed x27, local copies, waits for them, and re-layouts  23.3 us
    reduce_scatter x1, waiting for transfers between devices, shards(): lax.psum_scatter(qkv_part[:, None, :].astype(jnp.bfloat16), 'dp', scatter...  21.8 us
  transfers between devices with their start and end apart: 5, of which 4 were waited for; matrix products, arithmetic and copies ran while one was open for 9% of the time, Pallas kernels for 0%

commit v1 on v0

--- a/solution.py
+++ b/solution.py
@@ -43,7 +43,9 @@
 
 
 def shards(tokens, cotangent, w_qkv, w_out, moment_qkv, second_qkv, moment_out, second_out):
-    rows = lax.all_gather(tokens, "mp", axis=0, tiled=True)
+    rows = jnp.concatenate(
+        lax.all_to_all(jnp.stack(lax.axis_size("mp") * [tokens], axis=0), "mp", 0, 0), 0
+    )
     cot_rows = lax.all_gather(cotangent, "mp", axis=0, tiled=True)
     projection = w_qkv[:, 0, :]
     out_rows = w_out[0]

time: 928 us -> 790 us (0.85)
  waiting for transfers between devices: 822 us -> 481 us
  blocking collectives: 0 us -> 198 us
    all_gather x1 -> x0, waiting for transfers between devices: 277 us -> none  [shards(): rows = lax.all_gather(tokens, 'mp', axis=0, tiled=True)]
    all_to_all x0 -> x1, blocking collectives: none -> 198 us  [shards(): lax.all_to_all(jnp.stack(lax.axis_size('mp') * [tokens], axis=0), 'mp', 0...]
    all_gather x1, waiting for transfers between devices: 261 us -> 194 us  [shards(): cot_rows = lax.all_gather(cotangent, 'mp', axis=0, tiled=True)]
    unnamed x27 -> x29, local copies, waits for them, and re-layouts: 23.3 us -> 23.2 us
  transfers between devices with their start and end apart: 5 -> 4, of which waited for: 4 -> 3; matrix products, arithmetic and copies ran while one was open for 9% -> 11% of each run, Pallas kernels for 0% -> 0%
where the time goes in v1:
time: 790 us; the launch traced here: 789 us
  waiting for transfers between devices  481 us (61%)
  blocking collectives  198 us (25%)
  matrix products  52.5 us (7%)
  local copies, waits for them, and re-layouts  30.4 us (4%)
  between operations  14.1 us (2%)
  other arithmetic  12.1 us (2%)
    reduce_scatter x1, waiting for transfers between devices, shards(): lax.psum_scatter(whole_term.astype(jnp.bfloat16), 'mp', scatter_dimension...  261 us
    all_to_all x1, blocking collectives, shards(): lax.all_to_all(jnp.stack(lax.axis_size('mp') * [tokens], axis=0), 'mp', 0...  198 us
    all_gather x1, waiting for transfers between devices, shards(): cot_rows = lax.all_gather(cotangent, 'mp', axis=0, tiled=True)  194 us
    reduce_scatter x1, waiting for transfers between devices, shards(): lax.psum_scatter(qkv_part[:, None, :].astype(jnp.bfloat16), 'dp', scatter...  25.2 us
    unnamed x29, local copies, waits for them, and re-layouts  23.2 us
  transfers between devices with their start and end apart: 4, of which 3 were waited for; matrix products, arithmetic and copies ran while one was open for 11% of the time, Pallas kernels for 0%

profile of v1, /device:TPU:0, one launch (start us, length us, event | category | flops | bytes accessed | tf_op | source)
XLA Modules:
  0.0 789.0 jit_solution(6619462740013482106)
XLA Ops:
  8.0 7.2 stack.2
  15.1 198.0 %all_to_all.5 = bf16[32,64,3072]{2,1,0:T(8,128)(2,1)S(1)} all-to-all(bf16[32,64,3072]{2,1,0:T(8,128)(2,1)} %stack.2), channel_id=1, replica_groups=mesh['dp'=4,'mp'=32] {'mp'}, dimensions={0} | all-to-all | bytes 25165824 | tf_op jit(solution)/shard_map/all_to_all | solution.py:47
  213.1 6.7 bitcast_convert_fusion
  221.9 2.8 fusion.29
  224.8 1.4 copy-done.5
  226.7 194.5 %all-gather.2.cloned.1.call-done = bf16[2048,3072]{1,0:T(8,128)(2,1)} async-done(((bf16[64,3072]{1,0:T(8,128)(2,1)}), bf16[2048,3072]{1,0:T(8,128)(2,1)}) %all-gather.2.cloned.1.call-update) | async-done | bytes 12582928 | tf_op jit(solution)/shard_map/all_gather | solution.py:49
  421.1 7.3 fusion.1
  428.7 8.3 %convolution_convert_fusion.4 = bf16[2048,128]{1,0:T(8,128)(2,1)S(1)} fusion(bf16[2048,3072]{1,0:T(8,128)(2,1)} %all-gather.2.cloned.1.call-done, bf16[1,128,3072]{2,1,0:T(8,128)(2,1)} %param.11), kind=kOutput, calls=%fused_computation.7 | convolution fusion | flops 1610874880 | bytes 13893632 | tf_op jit(solution)/shard_map/dot_general | solution.py:55
  437.0 1.6 multiply_reduce_fusion
  439.0 3.1 multiply_reduce_fusion.2
  442.2 4.0 fusion.23
  446.2 1.3 fusion.24
  447.5 2.6 broadcast_add_fusion.1
  451.9 6.4 fusion
  458.6 11.2 %convolution_convert_fusion = bf16[2048,3072]{1,0:T(8,128)(2,1)} fusion(bf16[2048,384]{1,0:T(8,128)(2,1)} %bitcast.36, bf16[3072,1,384]{2,0,1:T(8,128)(2,1)S(1)} %copy-done), kind=kOutput, calls=%fused_computation | convolution fusion | flops 4838129664 | bytes 16515072 | tf_op jit(solution)/shard_map/dot_general | solution.py:59
  469.9 3.4 copy.16
  473.3 4.8 copy.17
  478.1 2.4 add_divide_fusion.1
  480.4 25.2 %reduce-scatter.6.cloned.1.call-done = bf16[768,1,384]{0,2,1:T(8,128)(2,1)} async-done(((bf16[3072,1,384]{0,2,1:T(8,128)(2,1)}), bf16[768,1,384]{0,2,1:T(8,128)(2,1)}) %reduce-scatter.6.cloned.1.call-update) | async-done | bytes 589840 | tf_op jit(solution)/shard_map/reduce_scatter | solution.py:64
  505.6 3.7 add_divide_fusion
  509.3 4.8 copy.19
  514.0 4.7 copy.20
  518.8 2.6 copy.21
  521.4 261.0 %reduce-scatter.4.cloned.1.call-done = bf16[64,3072]{1,0:T(8,128)(2,1)} async-done(((bf16[2048,3072]{1,0:T(8,128)(2,1)}), bf16[64,3072]{1,0:T(8,128)(2,1)}) %reduce-scatter.4.cloned.1.call-update) | async-done | bytes 393232 | tf_op jit(solution)/shard_map/reduce_scatter | solution.py:60
  (47 shorter events, 6.0 us)
Async XLA Ops:
  7.2 206.0 %copy-start = (bf16[3072,1,384]{2,0,1:T(8,128)(2,1)S(1)}, bf16[3072,1,384]{2,0,1:T(8,128)(2,1)}, u32[]{:S(2)}) copy-start(bf16[3072,1,384]{2,0,1:T(8,128)(2,1)} %param.10) | copy-start | bytes 7077892
  7.2 413.9 %all-gather.2.cloned.1.call-start = ((), (), s32[]{:S(2)}) async-start(), calls=%async_computation.4 | async-start | bytes 12976128 | tf_op jit(solution)/shard_map/all_gather | solution.py:49
  7.9 470.1 %reduce-scatter.8.cloned.1.call-start = ((), (), s32[]{:S(2)}) async-start(), calls=%async_computation.7 | async-start | bytes 983040 | tf_op jit(solution)/shard_map/reduce_scatter | solution.py:67
  213.1 6.7 copy-start.3
  219.9 2.0 copy-start.1
  219.9 4.8 copy-start.8
  224.7 1.4 copy-start.5
  428.4 77.2 %reduce-scatter.6.cloned.1.call-start = ((), (), s32[]{:S(2)}) async-start(), calls=%async_computation.6 | async-start | bytes 2949120 | tf_op jit(solution)/shard_map/reduce_scatter | solution.py:64
  428.6 8.3 %copy-start.6 = (f32[8,256,256]{1,2,0:T(8,128)S(1)}, f32[8,256,256]{1,2,0:T(8,128)}, u32[]{:S(2)}) copy-start(f32[8,256,256]{1,2,0:T(8,128)} %copy-done.5) | copy-start | bytes 6291460
  437.0 2.0 copy-start.2
  442.1 9.8 %slice-start = ((s8[12582912]{0:T(1024)(128)(4,1)}), s8[4194304]{0:T(1024)(128)(4,1)S(1)}, s32[]{:S(2)}) async-start(s8[12582912]{0:T(1024)(128)(4,1)} %bitcast.32), calls=%async_computation.8 | async-start | bytes 8388608
  442.1 9.7 %slice-start.1 = ((s8[12582912]{0:T(1024)(128)(4,1)}), s8[4194304]{0:T(1024)(128)(4,1)S(1)}, s32[]{:S(2)}) async-start(s8[12582912]{0:T(1024)(128)(4,1)} %bitcast.32), calls=%async_computation.9 | async-start | bytes 8388608
  447.5 4.4 slice-start.2
  450.7 1.2 copy-start.7
  458.4 324.1 %reduce-scatter.4.cloned.1.call-start = ((), (), s32[]{:S(2)}) async-start(), calls=%async_computation.5 | async-start | bytes 12976128 | tf_op jit(solution)/shard_map/reduce_scatter | solution.py:60
  509.3 9.5 %copy-start.4 = (f32[768,1,384]{0,2,1:T(8,128)S(1)}, f32[768,1,384]{0,2,1:T(8,128)}, u32[]{:S(2)}) copy-start(f32[768,1,384]{0,2,1:T(8,128)} %get-tuple-element.23) | copy-start | bytes 3538948
Sparse Core Ops, SparseCore 0:
  9.7 411.3 all-gather.1
  428.5 34.8 reduce-scatter.7
  466.2 39.3 reduce-scatter.5
  508.5 273.9 reduce-scatter.3
